TPU v7x, 256 devices: a whole 4x4x8 slice. The times are simulated.
256 devices in a mesh: samp: 32 (over x, z), snp: 8 (over y, core).
Axes of the slice: x: 4, y: 4, z: 8, core: 2. Of those that a mesh axis runs over, the one named last changes fastest.
Arguments:
- dosages: float32 [49152, 8192], P('samp', 'snp'), as said below
- band_counts: int32 [16], P('snp'), may hold values from 1 to 4, as said below
Outputs:
- corr_tiles: float32 [512, 16, 4, 512], P('samp', 'snp')
Inputs may be any that keep to these rules, and one draw needn't show every extreme that they name: b + band_counts[b] <= 16 for every block b, and the counts of all blocks sum to exactly 32. `dosages`: finite real values.
All inputs are finite; a program needn't handle non-finite values.
Results may differ from a plain program's by a relative error of at most 0.0001.
Values sent between devices are 32-bit elements; how exact they have to be, the bound alone decides.
No kernel may reach another device: no remote copies, remote signals or barrier semaphores. Data moves between devices by JAX's collectives and lax.ppermute only.
A program may use at most 192 MiB of HBM per device.

v0:
```python
import jax
import jax.numpy as jnp
from jax import lax
from jax.sharding import PartitionSpec as P

MAXBAND = 4
HIGHEST_MODE = lax.Precision.HIGHEST
epsilon_value = 1e-06
transposed_dims = (((0,), (0,)), ((), ()))


def shifted(value, axis, steps):
    count = lax.axis_size(axis)
    first, last = (max(0, -steps), min(count, count - steps))
    return lax.ppermute(value, axis, [(source, source + steps) for source in range(first, last)])


def on_device(dosages, band_counts):
    samp_rows, column_total = dosages.shape
    blocks_here = band_counts.shape[0]
    block_width = column_total // blocks_here
    band_limit = MAXBAND
    sample_total = samp_rows * lax.axis_size("samp")
    own_rows = block_width // lax.axis_size("samp")
    inverse_total = 1.0 / sample_total
    column_sum = lax.psum(jnp.sum(dosages, axis=0), "samp")
    center = column_sum * inverse_total
    deviation = dosages - center
    square_sum = lax.psum(jnp.sum(deviation * deviation, axis=0), "samp")
    spread = square_sum * inverse_total
    scaled = deviation * lax.rsqrt(spread + epsilon_value)
    band_range = jnp.arange(band_limit, dtype=jnp.int32)
    live_mask = band_range[None, :] < band_counts[:, None]
    reach = (band_limit - 1 + blocks_here - 1) // blocks_here
    sources = [scaled]
    for offset in range(1, reach + 1):
        sources.append(shifted(scaled, "snp", -offset))
    row_list = []
    for local_block in range(blocks_here):
        left_panel = lax.dynamic_slice_in_dim(
            scaled, local_block * block_width, own_rows * lax.axis_size("samp"), 1
        )
        band_list = []
        for band_index in range(band_limit):
            column_block = local_block + band_index
            source = sources[column_block // blocks_here]
            column_start = column_block % blocks_here * block_width
            right_panel = source[:, column_start : column_start + block_width]
            band_list.append(
                lax.dot_general(
                    left_panel,
                    right_panel,
                    transposed_dims,
                    precision=HIGHEST_MODE,
                    preferred_element_type=jnp.float32,
                )
            )
        row_list.append(jnp.stack(band_list, axis=1))
    tile_term = jnp.stack(row_list, axis=1) * inverse_total
    return lax.psum_scatter(
        jnp.where(live_mask[None, :, :, None], tile_term, 0.0),
        "samp",
        scatter_dimension=0,
        tiled=True,
    )


def solution(mesh):
    return jax.shard_map(
        on_device,
        mesh=mesh,
        in_specs=(P("samp", "snp"), P("snp")),
        out_specs=P("samp", "snp", None, None),
        check_vma=False,
    )
```

profile of v0, /device:TPU:8, one launch (start us, length us, event | category | flops | bytes accessed | tf_op | source)
XLA Modules:
  0.0 615.3 jit_solution(15016068143628533306)
XLA Ops:
  6.5 0.0 reduce-scatter.2.cloned.1.call-start
  6.5 3.2 reduce_sum.18
  9.7 77.7 %psum.14 = f32[1024]{0:T(1024)S(1)} all-reduce(f32[1024]{0:T(1024)S(1)} %reduce_sum.18), channel_id=1, replica_groups=mesh['samp'=32,'snp'=8] {'samp'}, use_global_device_ids=true, to_apply=%region_1.0 | all-reduce | flops 1024 | bytes 8192 | tf_op jit(solution)/shard_map/psum | solution.py:26
  87.4 3.5 multiply_reduce_fusion
  90.9 69.6 %psum.15 = f32[1024]{0:T(1024)S(1)} all-reduce(f32[1024]{0:T(1024)S(1)} %multiply_reduce_fusion), channel_id=1, replica_groups=mesh['samp'=32,'snp'=8] {'samp'}, use_global_device_ids=true, to_apply=%region_3.0 | all-reduce | flops 1024 | bytes 8192 | tf_op jit(solution)/shard_map/psum | solution.py:29
  160.5 0.0 copy-start
  160.5 3.6 subtract_multiply_fusion
  164.1 1.9 collective-permute-start
  166.1 2.1 collective-permute-start.1
  168.2 0.0 copy-done
  168.2 0.1 iota_compare_fusion
  168.2 5.3 fusion.26
  173.6 5.3 fusion.23
  178.9 5.5 fusion.29
  184.4 115.6 %collective-permute-done = f32[1536,1024]{1,0:T(8,128)S(1)} collective-permute-done((f32[1536,1024]{1,0:T(8,128)S(1)}, f32[1536,1024]{1,0:T(8,128)S(1)}, u32[]{:S(2)}, u32[]{:S(2)}) %collective-permute-start) | collective-permute-done | bytes 6291488 | tf_op jit(solution)/shard_map/ppermute | solution.py:15
  300.0 5.3 fusion.34
  305.3 5.7 fusion.44
  311.0 0.4 maximum_bitcast_fusion
  311.5 5.3 fusion.39
  316.7 5.5 fusion.49
  322.2 49.2 %collective-permute-done.1 = f32[1536,1024]{1,0:T(8,128)S(1)} collective-permute-done((f32[1536,1024]{1,0:T(8,128)S(1)}, f32[1536,1024]{1,0:T(8,128)S(1)}, u32[]{:S(2)}, u32[]{:S(2)}) %collective-permute-start.1) | collective-permute-done | bytes 6291488 | tf_op jit(solution)/shard_map/ppermute | solution.py:15
  371.4 5.3 fusion.54
  376.7 0.4 maximum_bitcast_fusion.1
  377.1 4.0 fusion
  381.2 0.0 reduce-scatter.2.cloned.1.call-update
  381.2 225.3 %reduce-scatter.2.cloned.1.call-done = f32[16,2,4,512]{3,0,2,1:T(8,128)} async-done(((f32[512,2,4,512]{3,0,2,1:T(8,128)}), f32[16,2,4,512]{3,0,2,1:T(8,128)}) %reduce-scatter.2.cloned.1.call-update) | async-done | bytes 262160 | tf_op jit(solution)/shard_map/reduce_scatter | solution.py:60
  606.5 1.8 copy.3
  (2 shorter events, 0.0 us)
Async XLA Ops:
  6.5 599.9 %reduce-scatter.2.cloned.1.call-start = ((), (), s32[]{:S(2)}) async-start(), calls=%async_computation.1 | async-start | bytes 8650752 | tf_op jit(solution)/shard_map/reduce_scatter | solution.py:60
  160.5 7.6 %copy-start = (s32[2]{0:T(128)S(1)}, s32[2]{0:T(128)}, u32[]{:S(2)}) copy-start(s32[2]{0:T(128)} %param.3) | copy-start | bytes 28
  164.1 135.9 %collective-permute-start = (f32[1536,1024]{1,0:T(8,128)S(1)}, f32[1536,1024]{1,0:T(8,128)S(1)}, u32[]{:S(2)}, u32[]{:S(2)}) collective-permute-start(f32[1536,1024]{1,0:T(8,128)S(1)} %subtract_multiply_fusion), channel_id=1, source_target_pairs={{1,0},{2,1},{3,2},{4,3},{5,4},{6,5},{7,6},{9,8},{10,9},{11,10},{12... | collective-permute-start | bytes 18874376 | tf_op jit(solution)/shard_map/ppermute | solution.py:15
  166.1 205.3 %collective-permute-start.1 = (f32[1536,1024]{1,0:T(8,128)S(1)}, f32[1536,1024]{1,0:T(8,128)S(1)}, u32[]{:S(2)}, u32[]{:S(2)}) collective-permute-start(f32[1536,1024]{1,0:T(8,128)S(1)} %subtract_multiply_fusion), channel_id=1, source_target_pairs={{2,0},{3,1},{4,2},{5,3},{6,4},{7,5},{10,8},{11,9},{12,10},{13,11},... | collective-permute-start | bytes 18874376 | tf_op jit(solution)/shard_map/ppermute | solution.py:15
Sparse Core Ops, SparseCore 0:
  381.3 225.0 reduce-scatter.1
where the time goes:
time: 619 us; the launch traced here: 615 us
  waiting for transfers between devices  390 us (63%)
  blocking collectives  147 us (24%)
  matrix products  43.2 us (7%)
  other arithmetic  15.3 us (2%)
  between operations  13.7 us (2%)
    reduce_scatter x1, waiting for transfers between devices, on_device(): lax.psum_scatter(jnp.where(live_mask[None, :, :, None], tile_term, 0.0),...  225 us
    ppermute x2, waiting for transfers between devices, shifted(): lax.ppermute(value, axis, [(source, source + steps) for source in range(f...  165 us
    psum x1, blocking collectives, on_device(): column_sum = lax.psum(jnp.sum(dosages, axis=0), 'samp')  77.7 us
    psum x1, blocking collectives, on_device(): square_sum = lax.psum(jnp.sum(deviation * deviation, axis=0), 'samp')  69.6 us
    dot_general x8, matrix products, on_device(): lax.dot_general(left_panel, right_panel, transposed_dims, precision=HIGHE...  43.2 us
  transfers between devices with their start and end apart: 3, of which 3 were waited for; matrix products, arithmetic and copies ran while one was open for 6% of the time, Pallas kernels for 0%

commit v1 on v0

--- a/solution.py
+++ b/solution.py
@@ -1,3 +1,4 @@
+import functools
 import jax
 import jax.numpy as jnp
 from jax import lax
@@ -7,6 +8,14 @@
 HIGHEST_MODE = lax.Precision.HIGHEST
 epsilon_value = 1e-06
 transposed_dims = (((0,), (0,)), ((), ()))
+
+
+def floor_perform(message, mesh_dim):
+    local_out = lax.all_gather(message, mesh_dim).sum(axis=0)
+    return local_out
+
+
+see_halves = functools.partial(floor_perform, mesh_dim="samp")
 
 
 def shifted(value, axis, steps):
@@ -23,7 +32,7 @@
     sample_total = samp_rows * lax.axis_size("samp")
     own_rows = block_width // lax.axis_size("samp")
     inverse_total = 1.0 / sample_total
-    column_sum = lax.psum(jnp.sum(dosages, axis=0), "samp")
+    column_sum = see_halves(jnp.sum(dosages, axis=0))
     center = column_sum * inverse_total
     deviation = dosages - center
     square_sum = lax.psum(jnp.sum(deviation * deviation, axis=0), "samp")

time: 619 us -> 590 us (0.953)
  blocking collectives: 147 us -> 119 us
    psum x1 -> x0, blocking collectives: 77.7 us -> none  [on_device(): column_sum = lax.psum(jnp.sum(dosages, axis=0), 'samp')]
    all_gather x0 -> x1, blocking collectives: none -> 46.4 us  [floor_perform(): local_out = lax.all_gather(message, mesh_dim).sum(axis=0)]
  transfers between devices with their start and end apart: 3 -> 3, of which waited for: 3 -> 3; matrix products, arithmetic and copies ran while one was open for 6% -> 7% of each run, Pallas kernels for 0% -> 0%
where the time goes in v1:
time: 590 us; the launch traced here: 586 us
  waiting for transfers between devices  389 us (66%)
  blocking collectives  119 us (20%)
  matrix products  43.2 us (7%)
  other arithmetic  15.3 us (3%)
  between operations  13.7 us (2%)
    reduce_scatter x1, waiting for transfers between devices, on_device(): lax.psum_scatter(jnp.where(live_mask[None, :, :, None], tile_term, 0.0),...  224 us
    ppermute x2, waiting for transfers between devices, shifted(): lax.ppermute(value, axis, [(source, source + steps) for source in range(f...  165 us
    psum x1, blocking collectives, on_device(): square_sum = lax.psum(jnp.sum(deviation * deviation, axis=0), 'samp')  72.3 us
    all_gather x1, blocking collectives, floor_perform(): local_out = lax.all_gather(message, mesh_dim).sum(axis=0)  46.4 us
    dot_general x8, matrix products, on_device(): lax.dot_general(left_panel, right_panel, transposed_dims, precision=HIGHE...  43.2 us
  transfers between devices with their start and end apart: 3, of which 3 were waited for; matrix products, arithmetic and copies ran while one was open for 7% of the time, Pallas kernels for 0%

profile of v1, /device:TPU:8, one launch (start us, length us, event | category | flops | bytes accessed | tf_op | source)
XLA Modules:
  0.0 585.6 jit_solution(4597458159385361926)
XLA Ops:
  6.5 0.0 reduce-scatter.2.cloned.1.call-start
  6.5 3.2 reduce_sum.27
  9.7 46.4 %all-gather = f32[32768]{0:T(1024)S(1)} all-gather(f32[1024]{0:T(1024)S(1)} %reduce_sum.27), channel_id=2, replica_groups=mesh['samp'=32,'snp'=8] {'samp'}, dimensions={0}, use_global_device_ids=true | all-gather | bytes 135168 | tf_op jit(solution)/shard_map/all_gather | solution.py:14
  56.2 3.5 multiply_reduce_fusion
  59.7 72.3 %psum.7 = f32[1024]{0:T(1024)S(1)} all-reduce(f32[1024]{0:T(1024)S(1)} %multiply_reduce_fusion), channel_id=1, replica_groups=mesh['samp'=32,'snp'=8] {'samp'}, use_global_device_ids=true, to_apply=%region_3.0 | all-reduce | flops 1024 | bytes 8192 | tf_op jit(solution)/shard_map/psum | solution.py:38
  132.0 0.0 copy-start
  132.0 3.6 subtract_multiply_fusion
  135.6 1.9 collective-permute-start
  137.5 2.1 collective-permute-start.1
  139.6 0.0 copy-done
  139.6 0.1 iota_compare_fusion
  139.7 5.3 fusion.26
  145.0 5.3 fusion.23
  150.4 5.5 fusion.29
  155.9 115.6 %collective-permute-done = f32[1536,1024]{1,0:T(8,128)S(1)} collective-permute-done((f32[1536,1024]{1,0:T(8,128)S(1)}, f32[1536,1024]{1,0:T(8,128)S(1)}, u32[]{:S(2)}, u32[]{:S(2)}) %collective-permute-start) | collective-permute-done | bytes 6291488 | tf_op jit(solution)/shard_map/ppermute | solution.py:24
  271.5 5.3 fusion.34
  276.8 5.7 fusion.44
  282.5 0.4 maximum_bitcast_fusion
  282.9 5.3 fusion.39
  288.2 5.5 fusion.49
  293.7 49.2 %collective-permute-done.1 = f32[1536,1024]{1,0:T(8,128)S(1)} collective-permute-done((f32[1536,1024]{1,0:T(8,128)S(1)}, f32[1536,1024]{1,0:T(8,128)S(1)}, u32[]{:S(2)}, u32[]{:S(2)}) %collective-permute-start.1) | collective-permute-done | bytes 6291488 | tf_op jit(solution)/shard_map/ppermute | solution.py:24
  342.8 5.3 fusion.54
  348.2 0.4 maximum_bitcast_fusion.1
  348.6 4.0 fusion
  352.6 0.0 reduce-scatter.2.cloned.1.call-update
  352.7 224.1 %reduce-scatter.2.cloned.1.call-done = f32[16,2,4,512]{3,0,2,1:T(8,128)} async-done(((f32[512,2,4,512]{3,0,2,1:T(8,128)}), f32[16,2,4,512]{3,0,2,1:T(8,128)}) %reduce-scatter.2.cloned.1.call-update) | async-done | bytes 262160 | tf_op jit(solution)/shard_map/reduce_scatter | solution.py:69
  576.8 1.8 copy.5
  (4 shorter events, 0.1 us)
Async XLA Ops:
  6.5 570.2 %reduce-scatter.2.cloned.1.call-start = ((), (), s32[]{:S(2)}) async-start(), calls=%async_computation.1 | async-start | bytes 8650752 | tf_op jit(solution)/shard_map/reduce_scatter | solution.py:69
  132.0 7.6 %copy-start = (s32[2]{0:T(128)S(1)}, s32[2]{0:T(128)}, u32[]{:S(2)}) copy-start(s32[2]{0:T(128)} %param.3) | copy-start | bytes 28
  135.6 135.9 %collective-permute-start = (f32[1536,1024]{1,0:T(8,128)S(1)}, f32[1536,1024]{1,0:T(8,128)S(1)}, u32[]{:S(2)}, u32[]{:S(2)}) collective-permute-start(f32[1536,1024]{1,0:T(8,128)S(1)} %subtract_multiply_fusion), channel_id=1, source_target_pairs={{1,0},{2,1},{3,2},{4,3},{5,4},{6,5},{7,6},{9,8},{10,9},{11,10},{12... | collective-permute-start | bytes 18874376 | tf_op jit(solution)/shard_map/ppermute | solution.py:24
  137.5 205.3 %collective-permute-start.1 = (f32[1536,1024]{1,0:T(8,128)S(1)}, f32[1536,1024]{1,0:T(8,128)S(1)}, u32[]{:S(2)}, u32[]{:S(2)}) collective-permute-start(f32[1536,1024]{1,0:T(8,128)S(1)} %subtract_multiply_fusion), channel_id=1, source_target_pairs={{2,0},{3,1},{4,2},{5,3},{6,4},{7,5},{10,8},{11,9},{12,10},{13,11},... | collective-permute-start | bytes 18874376 | tf_op jit(solution)/shard_map/ppermute | solution.py:24
Sparse Core Ops, SparseCore 0:
  352.8 223.9 reduce-scatter.1
